TPU v7x, 32 devices: a whole 2x2x4 slice. The times are simulated.
32 devices in a mesh: groups: 2 (over x), wide: 4 (over y, core), expert: 4 (over z).
Axes of the slice: x: 2, y: 2, z: 4, core: 2. Of those that a mesh axis runs over, the one named last changes fastest.
Arguments:
- prompts: bfloat16 [8, 128, 6144], P(('groups', 'wide'), None, 'expert'), parts along dimension 0, may hold values from -6 to 6
- span_slot_owner: int32 [8], P('groups'), parts along dimension 0, may hold values from 0 to 3, as said below
- row_expert_index: int32 [768, 2], P('groups'), parts along dimension 0, may hold values from 0 to 7, all different within a row
- tile_tenant_index: int32 [6], P('groups'), parts along dimension 0, may hold values from 0 to 7
- tenant_adapter_slot: int32 [16], P('groups'), parts along dimension 0, may hold values from 0 to 7, each once
- router: bfloat16 [6144, 8], replicated, may hold values from -0.078125 to 0.078125
- gate_weight: bfloat16 [2, 6144, 16384], P(None, None, ('wide', 'expert')), may hold values from -0.078125 to 0.078125
- up_weight: bfloat16 [2, 6144, 16384], P(None, None, ('wide', 'expert')), may hold values from -0.078125 to 0.078125
- down_weight: bfloat16 [2, 16384, 6144], P(None, 'wide', 'expert'), may hold values from -0.046875 to 0.046875
- adapter_down_weight: bfloat16 [16, 2, 6144, 64], P(('groups', 'wide'), None, 'expert'), parts along dimension 0, may hold values from -0.078125 to 0.078125
- adapter_up_weight: bfloat16 [16, 2, 64, 16384], P('groups', None, None, ('wide', 'expert')), parts along dimension 0, may hold values from -0.75 to 0.75
Outputs:
- mixed: bfloat16 [768, 6144], P(('groups', 'wide'), 'expert'), parts along dimension 0
There are 2 independent parts, one for each index of `groups`. A program takes and returns all parts, laid end to end along the dimension named above; an argument that names none is the same for every part. Nothing has to cross between parts.
Inputs may be any that keep to these rules, and one draw needn't show every extreme that they name: `span_slot_owner`: a permutation of the slots; span c, for c < 3, is in slot span_slot_owner[c]. `row_expert_index`: each row names two different experts. `tenant_adapter_slot`: a permutation of the slots. `tile_tenant_index`: tenant of rows 128 * i to 128 * i + 127.
All inputs are finite; a program needn't handle non-finite values.
Results may differ from a plain program's by a relative error of at most 0.0051.
Values may be sent and summed in bfloat16 or wider, within the bound.
No kernel may reach another device: no remote copies, remote signals or barrier semaphores. Data moves between devices by JAX's collectives and lax.ppermute only.
A program may use at most 128 MiB of HBM per device.

v0:
```python
import jax
import jax.numpy as jnp
import numpy as np
from jax import lax
from jax.sharding import Mesh
from jax.sharding import PartitionSpec as P

ADAPTER_SCALE = 0.5
WIDE = ("wy", "wc")
GROUP = ("wy", "wc", "expert")


def per_device(
    prompts,
    span_slot_owner,
    row_expert_index,
    tile_tenant_index,
    tenant_adapter_slot,
    router,
    gate_weight,
    up_weight,
    down_weight,
    adapter_down_weight,
    adapter_up_weight,
):
    span = prompts.shape[1]
    quarter = prompts.shape[2]
    tokens = row_expert_index.shape[0]
    nchunk = tokens // span
    window = gate_weight.shape[0]
    core = lax.axis_index("wc")
    cores = lax.axis_size("wc")
    wide_index = lax.axis_index(WIDE)
    slots_q = lax.all_gather(prompts, WIDE, axis=0, tiled=True)
    rows_q = jnp.take(slots_q, span_slot_owner[:nchunk], axis=0).reshape(tokens, quarter)
    half = tokens // cores
    mine_q = lax.dynamic_slice_in_dim(rows_q, core * half, half, 0)
    mine = lax.all_gather(mine_q, "expert", axis=1, tiled=True)
    other = lax.ppermute(mine, "wc", [(i, (i + 1) % cores) for i in range(cores)])
    first = jnp.where(core == 0, mine, other)
    second = jnp.where(core == 0, other, mine)
    input_rows = jnp.concatenate([first, second], axis=0)
    logits = jnp.dot(input_rows, router, preferred_element_type=jnp.float32)
    experts = jnp.arange(router.shape[1], dtype=jnp.int32)
    picked = (row_expert_index[:, :, None] == experts[None, None, :]).astype(jnp.float32)
    chosen = jnp.sum(picked * logits[:, None, :], axis=2)
    first_prob = jax.nn.sigmoid(chosen[:, 0] - chosen[:, 1])
    second_prob = jax.nn.sigmoid(chosen[:, 1] - chosen[:, 0])
    weight = (
        first_prob[:, None] * picked[:, 0, :window] + second_prob[:, None] * picked[:, 1, :window]
    )
    tile_count = tile_tenant_index.shape[0]
    tile_rows = tokens // tile_count
    resident_slots = adapter_down_weight.shape[0]
    tile_slot_index = jnp.take(tenant_adapter_slot, tile_tenant_index)
    owners = tile_slot_index // resident_slots
    local_index = tile_slot_index % resident_slots
    held = jnp.take(adapter_down_weight, local_index, axis=0)
    partial_rank = jnp.einsum(
        "ntd,nedr->nter",
        rows_q.reshape(tile_count, tile_rows, quarter),
        held,
        preferred_element_type=jnp.float32,
    )
    partial_rank = jnp.where(
        (owners == wide_index)[:, None, None, None], partial_rank, jnp.zeros_like(partial_rank)
    )
    lowrank = lax.reduce_precision(lax.psum(partial_rank, GROUP), exponent_bits=8, mantissa_bits=7)
    tile_up = jnp.take(adapter_up_weight, tile_tenant_index, axis=0)
    adapted_hidden = jnp.einsum(
        "nter,nerf->ntef", lowrank, tile_up.astype(jnp.float32), preferred_element_type=jnp.float32
    ).reshape(tokens, window, tile_up.shape[3])
    running = None
    for expert_number in range(window):
        gate_pre = jnp.dot(
            input_rows, gate_weight[expert_number], preferred_element_type=jnp.float32
        )
        up_value = (
            jnp.dot(input_rows, up_weight[expert_number], preferred_element_type=jnp.float32)
            + ADAPTER_SCALE * adapted_hidden[:, expert_number]
        )
        hidden = (weight[:, expert_number, None] * jax.nn.silu(gate_pre) * up_value).astype(
            jnp.bfloat16
        )
        gathered = lax.all_gather(hidden, "expert", axis=1, tiled=True)
        part = jnp.dot(gathered, down_weight[expert_number], preferred_element_type=jnp.float32)
        running = part if running is None else running + part
    mixed_rows = lax.psum_scatter(running, WIDE, scatter_dimension=0, tiled=True)
    return mixed_rows.astype(jnp.bfloat16)


def solution(mesh):
    groups = mesh.shape["groups"]
    wide = mesh.shape["wide"]
    expert = mesh.shape["expert"]
    split = Mesh(
        np.asarray(mesh.devices).reshape(groups, wide // 2, 2, expert),
        ("groups", "wy", "wc", "expert"),
    )
    rows = ("groups", "wy", "wc")
    in_specs = (
        P(rows, None, "expert"),
        P("groups"),
        P("groups", None),
        P("groups"),
        P("groups"),
        P(),
        P(None, None, GROUP),
        P(None, None, GROUP),
        P(None, WIDE, "expert"),
        P(rows, None, "expert", None),
        P("groups", None, None, GROUP),
    )
    out_specs = P(rows, "expert")
    return jax.shard_map(
        per_device, mesh=split, in_specs=in_specs, out_specs=out_specs, check_vma=False
    )
```

profile of v0, /device:TPU:0, one launch (start us, length us, event | category | flops | bytes accessed | tf_op | source)
XLA Modules:
  0.0 382.7 jit_solution(16340851096399354820)
XLA Ops:
  6.5 0.0 copy-start
  6.5 0.7 all-gather.5.cloned.1.call-update
  7.3 0.0 all-gather.7.cloned.1.call-start
  7.3 0.7 compare_and_fusion.2
  8.0 0.1 broadcast_bitcast_fusion
  8.1 0.1 dynamic-slice
  8.1 23.2 %all-gather.5.cloned.1.call-done = bf16[4,128,1536]{2,1,0:T(8,128)(2,1)} async-done(((bf16[1,128,1536]{2,1,0:T(8,128)(2,1)}), bf16[4,128,1536]{2,1,0:T(8,128)(2,1)}) %all-gather.5.cloned.1.call-update) | async-done | bytes 1572880 | tf_op jit(solution)/shard_map/all_gather | solution.py:34
  31.3 2.0 gather_fusion
  33.4 1.1 dynamic-slice_select_fusion
  34.5 0.0 all-gather.7.cloned.1.call-update
  34.5 0.0 all-reduce.2.cloned.1.call-start
  34.6 50.6 %all-gather.7.cloned.1.call-done = bf16[192,6144]{1,0:T(8,128)(2,1)} async-done(((bf16[192,1536]{1,0:T(8,128)(2,1)}), bf16[192,6144]{1,0:T(8,128)(2,1)}) %all-gather.7.cloned.1.call-update) | async-done | bytes 2359312 | tf_op jit(solution)/shard_map/all_gather | solution.py:38
  85.1 0.0 collective-permute-start
  85.1 0.0 copy-done.13
  85.2 0.6 gather_fusion.2
  85.9 0.0 copy-done.5
  85.9 1.8 gather_fusion.3
  87.7 0.2 broadcast_select_fusion.2
  87.8 0.0 copy-start.12
  87.8 1.1 copy-done.6
  88.9 0.5 fusion.33
  89.5 0.8 broadcast_select_fusion.3
  90.2 0.0 all-reduce.2.cloned.1.call-update
  90.2 0.0 all-gather.11.cloned.1.call-start
  90.3 0.6 gather_fusion.1
  90.9 88.2 %all-reduce.2.cloned.1.call-done = f32[3,128,2,64]{1,3,2,0:T(8,128)} async-done(((f32[3,128,2,64]{1,3,2,0:T(8,128)}), f32[3,128,2,64]{1,3,2,0:T(8,128)}) %all-reduce.2.cloned.1.call-update) | async-done | bytes 196624 | tf_op jit(solution)/shard_map/psum | solution.py:68
  179.1 1.6 convolution_bitcast_fusion
  180.7 0.4 copy.17
  181.1 0.0 copy-start.14
  181.1 0.0 collective-permute-done
  181.1 1.9 copy-done.7
  183.0 2.0 broadcast_select_fusion.1
  185.0 1.3 fusion.48
  186.4 8.1 %fusion.4 = f32[384,1024]{1,0:T(8,128)S(1)} fusion(bf16[2,6144,1024]{2,1,0:T(8,128)(2,1)} %param.17, bf16[192,6144]{1,0:T(8,128)(2,1)S(1)} %get-tuple-element.16, bf16[192,6144]{1,0:T(8,128)(2,1)S(1)} %get-tuple-element.15), kind=kOutput, calls=%fused_computation.8 | convolution fusion | flops 4841275392 | bytes 18874368 | tf_op jit(solution)/shard_map/dot_general | solution.py:75
  194.6 10.7 %fusion.24 = bf16[384,1024]{1,0:T(8,128)(2,1)} fusion(f32[384,2,1024]{2,0,1:T(8,128)S(1)} %bitcast.66, f32[384,1024]{1,0:T(8,128)S(1)} %fusion.4, bf16[2,6144,1024]{2,1,0:T(8,128)(2,1)} %param.18, f32[384]{0:T(512)S(1)} %get-tuple-element.6, bf16[192,6144]{1,0:T(8,128)(2,1)S(1)} %get-tuple-element.16, bf16[192,6144]{1,0:T(8,128)(2,1)S(1)} %get-tuple-element.15), kind=kOutput, calls=%fused_computation.31 | convolution fusion | flops 4844814336 | bytes 21235200 | tf_op jit(solution)/shard_map/dot_general | solution.py:79
  205.3 0.0 all-gather.11.cloned.1.call-update
  205.4 0.2 all-gather.9.cloned.1.call-start
  205.6 9.5 %fusion.10 = f32[384,1024]{1,0:T(8,128)S(1)} fusion(bf16[2,6144,1024]{2,1,0:T(8,128)(2,1)} %param.17, bf16[192,6144]{1,0:T(8,128)(2,1)} %copy-done.10, bf16[192,6144]{1,0:T(8,128)(2,1)} %copy-done.8), kind=kOutput, calls=%fused_computation.14 | convolution fusion | flops 4841275392 | bytes 18874368 | tf_op jit(solution)/shard_map/dot_general | solution.py:75
  215.2 10.8 %fusion.28 = bf16[384,1024]{1,0:T(8,128)(2,1)} fusion(f32[384,2,1024]{2,0,1:T(8,128)S(1)} %bitcast.67, f32[384,1024]{1,0:T(8,128)S(1)} %fusion.10, bf16[2,6144,1024]{2,1,0:T(8,128)(2,1)} %param.18, f32[384]{0:T(512)S(1)} %get-tuple-element.5, bf16[192,6144]{1,0:T(8,128)(2,1)S(1)} %copy-done.11, bf16[192,6144]{1,0:T(8,128)(2,1)S(1)} %copy-done.9), kind=kOutput, calls=%fused_computation.36 | convolution fusion | flops 4844814336 | bytes 21235200 | tf_op jit(solution)/shard_map/dot_general | solution.py:79
  226.0 0.0 all-gather.9.cloned.1.call-update
  226.0 0.0 reduce-scatter.2.cloned.1.call-start
  226.1 41.9 %all-gather.11.cloned.1.call-done = bf16[384,4096]{1,0:T(8,128)(2,1)} async-done(((bf16[384,1024]{1,0:T(8,128)(2,1)}), bf16[384,4096]{1,0:T(8,128)(2,1)}) %all-gather.11.cloned.1.call-update) | async-done | bytes 3145744 | tf_op jit(solution)/shard_map/all_gather | solution.py:85
  268.0 10.0 %fusion = f32[384,1536]{1,0:T(8,128)} fusion(bf16[384,4096]{1,0:T(8,128)(2,1)} %all-gather.11.cloned.1.call-done, bf16[2,4096,1536]{2,1,0:T(8,128)(2,1)} %param.19), kind=kOutput, calls=%fused_computation.4 | convolution fusion | flops 4831838208 | bytes 18087936 | tf_op jit(solution)/shard_map/dot_general | solution.py:86
  278.0 53.6 %all-gather.9.cloned.1.call-done = bf16[384,4096]{1,0:T(8,128)(2,1)} async-done(((bf16[384,1024]{1,0:T(8,128)(2,1)}), bf16[384,4096]{1,0:T(8,128)(2,1)}) %all-gather.9.cloned.1.call-update) | async-done | bytes 3145744 | tf_op jit(solution)/shard_map/all_gather | solution.py:85
  331.6 10.5 %fusion.18 = f32[384,1536]{1,0:T(8,128)} fusion(f32[384,1536]{1,0:T(8,128)} %fusion, bf16[384,4096]{1,0:T(8,128)(2,1)} %all-gather.9.cloned.1.call-done, bf16[2,4096,1536]{2,1,0:T(8,128)(2,1)} %param.19), kind=kOutput, calls=%fused_computation.23 | convolution fusion | flops 4832428032 | bytes 20447232 | tf_op jit(solution)/shard_map/dot_general | solution.py:86
  342.1 0.0 reduce-scatter.2.cloned.1.call-update
  342.1 31.9 %reduce-scatter.2.cloned.1.call-done = f32[96,1536]{1,0:T(8,128)} async-done(((f32[384,1536]{1,0:T(8,128)}), f32[96,1536]{1,0:T(8,128)}) %reduce-scatter.2.cloned.1.call-update) | async-done | bytes 589840 | tf_op jit(solution)/shard_map/reduce_scatter | solution.py:88
  374.0 1.8 convert_element_type.16
  (35 shorter events, 0.2 us)
Async XLA Ops:
  6.5 83.8 %copy-start = (bf16[8,2,64,1024]{3,2,1,0:T(8,128)(2,1)S(1)}, bf16[8,2,64,1024]{3,2,1,0:T(8,128)(2,1)}, u32[]{:S(2)}) copy-start(bf16[8,2,64,1024]{3,2,1,0:T(8,128)(2,1)} %param.21) | copy-start | bytes 6291460
  6.5 78.6 %copy-start.13 = (s32[3]{0:T(128)S(1)}, s32[3]{0:T(128)}, u32[]{:S(2)}) copy-start(s32[3]{0:T(128)} %param.14) | copy-start | bytes 40
  6.5 78.6 %copy-start.2 = (s32[8]{0:T(128)S(1)}, s32[8]{0:T(128)}, u32[]{:S(2)}) copy-start(s32[8]{0:T(128)} %param.15) | copy-start | bytes 100
  6.5 24.8 %all-gather.5.cloned.1.call-start = ((), (), s32[]{:S(2)}) async-start(), calls=%async_computation.1 | async-start | bytes 1966080 | tf_op jit(solution)/shard_map/all_gather | solution.py:34
  7.3 77.9 %all-gather.7.cloned.1.call-start = ((), (), s32[]{:S(2)}) async-start(), calls=%async_computation.2 | async-start | bytes 2949120 | tf_op jit(solution)/shard_map/all_gather | solution.py:38
  33.4 52.5 %copy-start.5 = (bf16[3,128,1536]{2,1,0:T(8,128)(2,1)}, bf16[3,128,1536]{2,1,0:T(8,128)(2,1)S(1)}, u32[]{:S(2)}) copy-start(bf16[3,128,1536]{2,1,0:T(8,128)(2,1)S(1)} %gather_fusion) | copy-start | bytes 3538948
  34.5 144.6 %all-reduce.2.cloned.1.call-start = ((), (), s32[]{:S(2)}) async-start(), calls=%async_computation.3 | async-start | bytes 393216 | tf_op jit(solution)/shard_map/psum | solution.py:68
  85.1 96.0 %collective-permute-start = (bf16[192,6144]{1,0:T(8,128)(2,1)}, bf16[192,6144]{1,0:T(8,128)(2,1)}, u32[]{:S(2)}, u32[]{:S(2)}) collective-permute-start(bf16[192,6144]{1,0:T(8,128)(2,1)} %all-gather.7.cloned.1.call-done), channel_id=1, source_target_pairs={{0,4},{4,0},{1,5},{5,1},{2,6},{6,2},{3,7},{7,3},{8,12},{12,8},{9,1... | collective-permute-start | bytes 7077896 | tf_op jit(solution)/shard_map/ppermute | solution.py:39
  87.6 1.3 copy-start.6
  87.8 2.5 copy-start.12
  90.2 177.7 %all-gather.11.cloned.1.call-start = ((), (), s32[]{:S(2)}) async-start(), calls=%async_computation.5 | async-start | bytes 3932160 | tf_op jit(solution)/shard_map/all_gather | solution.py:85
  180.7 2.3 copy-start.7
  181.1 13.5 %copy-start.3 = (f32[3,128,2,1024]{3,1,0,2:T(8,128)}, f32[3,128,2,1024]{3,1,0,2:T(8,128)S(1)}, u32[]{:S(2)}) copy-start(f32[3,128,2,1024]{3,1,0,2:T(8,128)S(1)} %copy.17) | copy-start | bytes 9437188
  181.1 3.9 %copy-start.14 = (bf16[6144,8]{0,1:T(8,128)(2,1)S(1)}, bf16[6144,8]{0,1:T(8,128)(2,1)}, u32[]{:S(2)}) copy-start(bf16[6144,8]{0,1:T(8,128)(2,1)} %param.16) | copy-start | bytes 294916
  185.0 9.6 %copy-start.8 = (bf16[192,6144]{1,0:T(8,128)(2,1)}, bf16[192,6144]{1,0:T(8,128)(2,1)S(1)}, u32[]{:S(2)}) copy-start(bf16[192,6144]{1,0:T(8,128)(2,1)S(1)} %get-tuple-element.15) | copy-start | bytes 7077892
  185.0 9.6 %copy-start.10 = (bf16[192,6144]{1,0:T(8,128)(2,1)}, bf16[192,6144]{1,0:T(8,128)(2,1)S(1)}, u32[]{:S(2)}) copy-start(bf16[192,6144]{1,0:T(8,128)(2,1)S(1)} %get-tuple-element.16) | copy-start | bytes 7077892
  205.4 126.2 %all-gather.9.cloned.1.call-start = ((), (), s32[]{:S(2)}) async-start(), calls=%async_computation.4 | async-start | bytes 3932160 | tf_op jit(solution)/shard_map/all_gather | solution.py:85
  205.6 9.6 %copy-start.4 = (f32[3,128,2,1024]{3,1,0,2:T(8,128)S(1)}, f32[3,128,2,1024]{3,1,0,2:T(8,128)}, u32[]{:S(2)}) copy-start(f32[3,128,2,1024]{3,1,0,2:T(8,128)} %copy-done.3) | copy-start | bytes 9437188
  205.6 9.6 %copy-start.9 = (bf16[192,6144]{1,0:T(8,128)(2,1)S(1)}, bf16[192,6144]{1,0:T(8,128)(2,1)}, u32[]{:S(2)}) copy-start(bf16[192,6144]{1,0:T(8,128)(2,1)} %copy-done.8) | copy-start | bytes 7077892
  205.6 9.6 %copy-start.11 = (bf16[192,6144]{1,0:T(8,128)(2,1)S(1)}, bf16[192,6144]{1,0:T(8,128)(2,1)}, u32[]{:S(2)}) copy-start(bf16[192,6144]{1,0:T(8,128)(2,1)} %copy-done.10) | copy-start | bytes 7077892
  226.0 148.0 %reduce-scatter.2.cloned.1.call-start = ((), (), s32[]{:S(2)}) async-start(), calls=%async_computation.6 | async-start | bytes 2949120 | tf_op jit(solution)/shard_map/reduce_scatter | solution.py:88
  331.6 44.3 %copy-start.1 = (bf16[8,2,64,1024]{3,2,1,0:T(8,128)(2,1)S(1)}, bf16[8,2,64,1024]{3,2,1,0:T(8,128)(2,1)}, u32[]{:S(2)}) copy-start(bf16[8,2,64,1024]{3,2,1,0:T(8,128)(2,1)} %param.21) | copy-start | bytes 6291460
Sparse Core Ops, SparseCore 0:
  8.9 22.3 all-gather.4
  34.6 50.4 all-gather.6
  90.4 88.7 all-reduce.1
  205.5 62.4 all-gather.10
  269.4 62.1 all-gather.8
  342.2 31.7 reduce-scatter.1
where the time goes:
time: 383 us
  waiting for transfers between devices  290 us (76%)
  matrix products  63.1 us (16%)
  between operations  13.8 us (4%)
  local copies, waits for them, and re-layouts  8.6 us (2%)
  other arithmetic  6.66 us (2%)
    all_gather x2, waiting for transfers between devices, per_device(): gathered = lax.all_gather(hidden, 'expert', axis=1, tiled=True)  95.5 us
    psum x1, waiting for transfers between devices, per_device(): lax.psum(partial_rank, GROUP)  88.2 us
    all_gather x1, waiting for transfers between devices, per_device(): mine = lax.all_gather(mine_q, 'expert', axis=1, tiled=True)  50.6 us
    reduce_scatter x1, waiting for transfers between devices, per_device(): lax.psum_scatter(running, WIDE, scatter_dimension=0, tiled=True)  31.9 us
    all_gather x1, waiting for transfers between devices, per_device(): slots_q = lax.all_gather(prompts, WIDE, axis=0, tiled=True)  23.2 us
    dot_general x2, matrix products, per_device(): jnp.dot(input_rows, up_weight[expert_number], preferred_element_type=jnp....  21.6 us
    dot_general x2, matrix products, per_device(): jnp.dot(gathered, down_weight[expert_number], preferred_element_type=jnp....  20.5 us
    dot_general x2, matrix products, per_device(): jnp.dot(input_rows, gate_weight[expert_number], preferred_element_type=jn...  17.7 us
  transfers between devices with their start and end apart: 7, of which 6 were waited for; matrix products, arithmetic and copies ran while one was open for 10% of the time, Pallas kernels for 0%

commit v1 on v0

--- a/solution.py
+++ b/solution.py
@@ -8,6 +8,19 @@
 ADAPTER_SCALE = 0.5
 WIDE = ("wy", "wc")
 GROUP = ("wy", "wc", "expert")
+
+
+def collect(value, axis, dim):
+    ways = lax.axis_size(axis)
+    up = [(d, (d + 1) % ways) for d in range(ways)]
+    down = [(d, (d - 1) % ways) for d in range(ways)]
+    earlier, later = ([value], [value])
+    for _ in range(ways // 2):
+        earlier.append(lax.ppermute(earlier[-1], axis, up))
+    for _ in range((ways - 1) // 2):
+        later.append(lax.ppermute(later[-1], axis, down))
+    line = jnp.concatenate([*earlier[::-1], *later[1:]], axis=dim)
+    return jnp.roll(line, (lax.axis_index(axis) - ways // 2) * value.shape[dim], axis=dim)
 
 
 def per_device(
@@ -82,7 +95,7 @@
         hidden = (weight[:, expert_number, None] * jax.nn.silu(gate_pre) * up_value).astype(
             jnp.bfloat16
         )
-        gathered = lax.all_gather(hidden, "expert", axis=1, tiled=True)
+        gathered = collect(hidden, "expert", 1)
         part = jnp.dot(gathered, down_weight[expert_number], preferred_element_type=jnp.float32)
         running = part if running is None else running + part
     mixed_rows = lax.psum_scatter(running, WIDE, scatter_dimension=0, tiled=True)

time: 383 us -> 371 us (0.969)
  waiting for transfers between devices: 290 us -> 253 us
  starting transfers between devices: 0.39 us -> 22.4 us
  matrix products: 63.1 us -> 67.7 us
    all_gather x2 -> x0, waiting for transfers between devices: 95.5 us -> none  [per_device(): gathered = lax.all_gather(hidden, 'expert', axis=1, tiled=True)]
    ppermute x0 -> x6, waiting for transfers between devices: none -> 60.2 us  [the longest x4 52.1 us: collect(): earlier.append(lax.ppermute(earlier[-1], axis, up))]
    ppermute x0 -> x6, starting transfers between devices: none -> 22.3 us  [the longest x4 15.2 us: collect(): earlier.append(lax.ppermute(earlier[-1], axis, up))]
    dot_general x2, matrix products: 20.5 us -> 27.2 us  [per_device(): jnp.dot(gathered, down_weight[expert_number], preferred_element_type=jnp....]
  transfers between devices with their start and end apart: 7 -> 11, of which waited for: 6 -> 10; matrix products, arithmetic and copies ran while one was open for 10% -> 8% of each run, Pallas kernels for 0% -> 0%
where the time goes in v1:
time: 371 us; the launch traced here: 370 us
  waiting for transfers between devices  253 us (68%)
  matrix products  67.7 us (18%)
  starting transfers between devices  22.4 us (6%)
  between operations  13.4 us (4%)
  local copies, waits for them, and re-layouts  6.87 us (2%)
  other arithmetic  6.75 us (2%)
    psum x1, waiting for transfers between devices, per_device(): lax.psum(partial_rank, GROUP)  88.2 us
    ppermute x4, waiting for transfers between devices, collect(): earlier.append(lax.ppermute(earlier[-1], axis, up))  52.1 us
    all_gather x1, waiting for transfers between devices, per_device(): mine = lax.all_gather(mine_q, 'expert', axis=1, tiled=True)  50.6 us
    reduce_scatter x1, waiting for transfers between devices, per_device(): lax.psum_scatter(running, WIDE, scatter_dimension=0, tiled=True)  30.5 us
    dot_general x2, matrix products, per_device(): jnp.dot(gathered, down_weight[expert_number], preferred_element_type=jnp....  27.2 us
    all_gather x1, waiting for transfers between devices, per_device(): slots_q = lax.all_gather(prompts, WIDE, axis=0, tiled=True)  23.2 us
    dot_general x2, matrix products, per_device(): jnp.dot(input_rows, up_weight[expert_number], preferred_element_type=jnp....  19.6 us
    dot_general x2, matrix products, per_device(): jnp.dot(input_rows, gate_weight[expert_number], preferred_element_type=jn...  16.1 us
  transfers between devices with their start and end apart: 11, of which 10 were waited for; matrix products, arithmetic and copies ran while one was open for 8% of the time, Pallas kernels for 0%

profile of v1, /device:TPU:0, one launch (start us, length us, event | category | flops | bytes accessed | tf_op | source)
XLA Modules:
  0.0 370.4 jit_solution(13584348068033215554)
XLA Ops:
  6.5 0.7 all-gather.3.cloned.1.call-update
  7.3 0.0 all-gather.5.cloned.1.call-start
  7.3 0.7 compare_and_fusion.2
  8.0 0.1 broadcast_bitcast_fusion
  8.1 0.1 dynamic-slice
  8.1 23.2 %all-gather.3.cloned.1.call-done = bf16[4,128,1536]{2,1,0:T(8,128)(2,1)} async-done(((bf16[1,128,1536]{2,1,0:T(8,128)(2,1)}), bf16[4,128,1536]{2,1,0:T(8,128)(2,1)}) %all-gather.3.cloned.1.call-update) | async-done | bytes 1572880 | tf_op jit(solution)/shard_map/all_gather | solution.py:47
  31.3 2.0 gather_fusion
  33.4 1.2 dynamic-slice_select_fusion
  34.6 0.0 all-gather.5.cloned.1.call-update
  34.6 0.0 all-reduce.2.cloned.1.call-start
  34.7 50.6 %all-gather.5.cloned.1.call-done = bf16[192,6144]{1,0:T(8,128)(2,1)} async-done(((bf16[192,1536]{1,0:T(8,128)(2,1)}), bf16[192,6144]{1,0:T(8,128)(2,1)}) %all-gather.5.cloned.1.call-update) | async-done | bytes 2359312 | tf_op jit(solution)/shard_map/all_gather | solution.py:51
  85.2 0.0 collective-permute-start
  85.3 0.6 gather_fusion.2
  86.0 1.8 gather_fusion.3
  87.7 0.0 copy-start.5
  87.7 0.2 broadcast_select_fusion.2
  87.9 1.8 fusion.53
  89.8 0.8 broadcast_select_fusion.3
  90.5 0.0 all-reduce.2.cloned.1.call-update
  90.5 0.0 reduce-scatter.2.cloned.1.call-start
  90.6 0.6 gather_fusion.1
  91.2 88.2 %all-reduce.2.cloned.1.call-done = f32[3,128,2,64]{1,3,2,0:T(8,128)} async-done(((f32[3,128,2,64]{1,3,2,0:T(8,128)}), f32[3,128,2,64]{1,3,2,0:T(8,128)}) %all-reduce.2.cloned.1.call-update) | async-done | bytes 196624 | tf_op jit(solution)/shard_map/psum | solution.py:81
  179.5 1.6 convolution_bitcast_fusion
  181.0 0.4 copy.17
  181.4 1.2 copy-done.4
  182.7 2.0 broadcast_select_fusion.1
  184.7 8.0 %fusion.10 = f32[384,1024]{1,0:T(8,128)S(1)} fusion(bf16[2,6144,1024]{2,1,0:T(8,128)(2,1)} %param.19, bf16[192,6144]{1,0:T(8,128)(2,1)S(1)} %get-tuple-element.17, bf16[192,6144]{1,0:T(8,128)(2,1)S(1)} %get-tuple-element.16), kind=kOutput, calls=%fused_computation.14 | convolution fusion | flops 4841275392 | bytes 18874368 | tf_op jit(solution)/shard_map/dot_general | solution.py:88
  192.7 0.0 copy-start.7
  192.7 8.1 %fusion.4 = f32[384,1024]{1,0:T(8,128)S(1)} fusion(bf16[2,6144,1024]{2,1,0:T(8,128)(2,1)} %param.19, bf16[192,6144]{1,0:T(8,128)(2,1)S(1)} %get-tuple-element.17, bf16[192,6144]{1,0:T(8,128)(2,1)S(1)} %get-tuple-element.16), kind=kOutput, calls=%fused_computation.8 | convolution fusion | flops 4841275392 | bytes 18874368 | tf_op jit(solution)/shard_map/dot_general | solution.py:88
  200.8 1.3 fusion.72
  202.2 9.8 %fusion.44 = bf16[384,1024]{1,0:T(8,128)(2,1)S(1)} fusion(f32[384,2,1024]{2,0,1:T(8,128)S(1)} %bitcast.64, f32[384,1024]{1,0:T(8,128)S(1)} %fusion.4, bf16[2,6144,1024]{2,1,0:T(8,128)(2,1)} %param.20, f32[384]{0:T(512)S(1)} %get-tuple-element.7, bf16[192,6144]{1,0:T(8,128)(2,1)S(1)} %get-tuple-element.17, bf16[192,6144]{1,0:T(8,128)(2,1)S(1)} %get-tuple-element.16), kind=kOutput, calls=%fused_computation.61 | convolution fusion | flops 4844814336 | bytes 21235200 | tf_op jit(solution)/shard_map/dot_general | solution.py:92
  212.0 1.6 collective-permute-start.4
  213.7 9.8 %fusion.48 = bf16[384,1024]{1,0:T(8,128)(2,1)S(1)} fusion(f32[384,2,1024]{2,0,1:T(8,128)S(1)} %bitcast.65, f32[384,1024]{1,0:T(8,128)S(1)} %fusion.10, bf16[2,6144,1024]{2,1,0:T(8,128)(2,1)} %param.20, f32[384]{0:T(512)S(1)} %get-tuple-element.6, bf16[192,6144]{1,0:T(8,128)(2,1)S(1)} %get-tuple-element.17, bf16[192,6144]{1,0:T(8,128)(2,1)S(1)} %get-tuple-element.16), kind=kOutput, calls=%fused_computation.66 | convolution fusion | flops 4844814336 | bytes 21235200 | tf_op jit(solution)/shard_map/dot_general | solution.py:92
  223.5 0.6 collective-permute-start.1
  224.1 3.3 collective-permute-start.6
  227.4 7.3 %collective-permute-done.4 = bf16[384,1024]{1,0:T(8,128)(2,1)S(1)} collective-permute-done((bf16[384,1024]{1,0:T(8,128)(2,1)S(1)}, bf16[384,1024]{1,0:T(8,128)(2,1)S(1)}, u32[]{:S(2)}, u32[]{:S(2)}) %collective-permute-start.4) | collective-permute-done | bytes 786464 | tf_op jit(solution)/shard_map/ppermute | solution.py:19
  234.7 3.8 %collective-permute-start.3 = (bf16[384,1024]{1,0:T(8,128)(2,1)S(1)}, bf16[384,1024]{1,0:T(8,128)(2,1)S(1)}, u32[]{:S(2)}, u32[]{:S(2)}) collective-permute-start(bf16[384,1024]{1,0:T(8,128)(2,1)S(1)} %fusion.48), channel_id=1, source_target_pairs={{0,3},{1,0},{2,1},{3,2},{4,7},{5,4},{6,5},{7,6},{8,11},{9,8},{10,9... | collective-permute-start | bytes 2359304 | tf_op jit(solution)/shard_map/ppermute | solution.py:21
  238.5 13.0 %collective-permute-done.1 = bf16[384,1024]{1,0:T(8,128)(2,1)} collective-permute-done((bf16[384,1024]{1,0:T(8,128)(2,1)S(1)}, bf16[384,1024]{1,0:T(8,128)(2,1)}, u32[]{:S(2)}, u32[]{:S(2)}) %collective-permute-start.1) | collective-permute-done | bytes 786464 | tf_op jit(solution)/shard_map/ppermute | solution.py:19
  251.5 13.0 %collective-permute-start.2 = (bf16[384,1024]{1,0:T(8,128)(2,1)}, bf16[384,1024]{1,0:T(8,128)(2,1)S(1)}, u32[]{:S(2)}, u32[]{:S(2)}) collective-permute-start(bf16[384,1024]{1,0:T(8,128)(2,1)} %collective-permute-done.1), channel_id=1, source_target_pairs={{0,1},{1,2},{2,3},{3,0},{4,5},{5,6},{6,7},{7,4},{8,9},{9,10},{10,1... | collective-permute-start | bytes 2359304 | tf_op jit(solution)/shard_map/ppermute | solution.py:19
  264.5 4.0 %collective-permute-done.6 = bf16[384,1024]{1,0:T(8,128)(2,1)} collective-permute-done((bf16[384,1024]{1,0:T(8,128)(2,1)S(1)}, bf16[384,1024]{1,0:T(8,128)(2,1)}, u32[]{:S(2)}, u32[]{:S(2)}) %collective-permute-start.6) | collective-permute-done | bytes 786464 | tf_op jit(solution)/shard_map/ppermute | solution.py:21
  268.6 16.7 %collective-permute-done.5 = bf16[384,1024]{1,0:T(8,128)(2,1)} collective-permute-done((bf16[384,1024]{1,0:T(8,128)(2,1)S(1)}, bf16[384,1024]{1,0:T(8,128)(2,1)}, u32[]{:S(2)}, u32[]{:S(2)}) %collective-permute-start.5) | collective-permute-done | bytes 786464 | tf_op jit(solution)/shard_map/ppermute | solution.py:19
  285.3 12.6 %fusion = f32[384,1536]{1,0:T(8,128)S(1)} fusion(bf16[2,4096,1536]{2,1,0:T(8,128)(2,1)} %param.21, s32[]{:T(128)S(6)} %select_n.110, bf16[384,1024]{1,0:T(8,128)(2,1)} %collective-permute-done.5, bf16[384,1024]{1,0:T(8,128)(2,1)S(1)} %collective-permute-done.4, bf16[384,1024]{1,0:T(8,128)(2,1)S(1)} %fusion.44, bf16[384,1024]{1,0:T(8,128)(2,1)} %collective-permute-done.6), kind=kOutput, calls=%fused_computation.4 | convolution fusion | flops 4857004032 | bytes 18087940 | tf_op jit(solution)/shard_map/dot_general | solution.py:99
  297.9 4.0 %collective-permute-done.3 = bf16[384,1024]{1,0:T(8,128)(2,1)S(1)} collective-permute-done((bf16[384,1024]{1,0:T(8,128)(2,1)S(1)}, bf16[384,1024]{1,0:T(8,128)(2,1)S(1)}, u32[]{:S(2)}, u32[]{:S(2)}) %collective-permute-start.3) | collective-permute-done | bytes 786464 | tf_op jit(solution)/shard_map/ppermute | solution.py:21
  301.9 15.0 %collective-permute-done.2 = bf16[384,1024]{1,0:T(8,128)(2,1)S(1)} collective-permute-done((bf16[384,1024]{1,0:T(8,128)(2,1)}, bf16[384,1024]{1,0:T(8,128)(2,1)S(1)}, u32[]{:S(2)}, u32[]{:S(2)}) %collective-permute-start.2) | collective-permute-done | bytes 786464 | tf_op jit(solution)/shard_map/ppermute | solution.py:19
  316.9 14.7 %fusion.36 = f32[384,1536]{1,0:T(8,128)} fusion(f32[384,1536]{1,0:T(8,128)S(1)} %fusion, bf16[2,4096,1536]{2,1,0:T(8,128)(2,1)} %param.21, s32[]{:T(128)S(6)} %select_n.110, bf16[384,1024]{1,0:T(8,128)(2,1)S(1)} %collective-permute-done.2, bf16[384,1024]{1,0:T(8,128)(2,1)} %collective-permute-done.1, bf16[384,1024]{1,0:T(8,128)(2,1)S(1)} %fusion.48, ...), kind=kOutput, calls=%fused_computation.53 | convolution fusion | flops 4857593856 | bytes 20447236 | tf_op jit(solution)/shard_map/dot_general | solution.py:99
  331.6 0.0 reduce-scatter.2.cloned.1.call-update
  331.6 30.5 %reduce-scatter.2.cloned.1.call-done = f32[96,1536]{1,0:T(8,128)} async-done(((f32[384,1536]{1,0:T(8,128)}), f32[96,1536]{1,0:T(8,128)}) %reduce-scatter.2.cloned.1.call-update) | async-done | bytes 589840 | tf_op jit(solution)/shard_map/reduce_scatter | solution.py:101
  362.1 1.8 convert_element_type.16
  (27 shorter events, 0.2 us)
Async XLA Ops:
  6.5 84.1 %copy-start = (bf16[8,2,64,1024]{3,2,1,0:T(8,128)(2,1)S(1)}, bf16[8,2,64,1024]{3,2,1,0:T(8,128)(2,1)}, u32[]{:S(2)}) copy-start(bf16[8,2,64,1024]{3,2,1,0:T(8,128)(2,1)} %param.23) | copy-start | bytes 6291460
  6.5 78.7 %copy-start.6 = (s32[3]{0:T(128)S(1)}, s32[3]{0:T(128)}, u32[]{:S(2)}) copy-start(s32[3]{0:T(128)} %param.16) | copy-start | bytes 40
  6.5 78.7 %copy-start.2 = (s32[8]{0:T(128)S(1)}, s32[8]{0:T(128)}, u32[]{:S(2)}) copy-start(s32[8]{0:T(128)} %param.17) | copy-start | bytes 100
  6.5 24.8 %all-gather.3.cloned.1.call-start = ((), (), s32[]{:S(2)}) async-start(), calls=%async_computation.1 | async-start | bytes 1966080 | tf_op jit(solution)/shard_map/all_gather | solution.py:47
  7.3 77.9 %all-gather.5.cloned.1.call-start = ((), (), s32[]{:S(2)}) async-start(), calls=%async_computation.2 | async-start | bytes 2949120 | tf_op jit(solution)/shard_map/all_gather | solution.py:51
  33.4 52.6 %copy-start.3 = (bf16[3,128,1536]{2,1,0:T(8,128)(2,1)}, bf16[3,128,1536]{2,1,0:T(8,128)(2,1)S(1)}, u32[]{:S(2)}) copy-start(bf16[3,128,1536]{2,1,0:T(8,128)(2,1)S(1)} %gather_fusion) | copy-start | bytes 3538948
  34.6 144.8 %all-reduce.2.cloned.1.call-start = ((), (), s32[]{:S(2)}) async-start(), calls=%async_computation.3 | async-start | bytes 393216 | tf_op jit(solution)/shard_map/psum | solution.py:81
  85.2 96.2 %collective-permute-start = (bf16[192,6144]{1,0:T(8,128)(2,1)}, bf16[192,6144]{1,0:T(8,128)(2,1)}, u32[]{:S(2)}, u32[]{:S(2)}) collective-permute-start(bf16[192,6144]{1,0:T(8,128)(2,1)} %all-gather.5.cloned.1.call-done), channel_id=1, source_target_pairs={{0,4},{4,0},{1,5},{5,1},{2,6},{6,2},{3,7},{7,3},{8,12},{12,8},{9,1... | collective-permute-start | bytes 7077896 | tf_op jit(solution)/shard_map/ppermute | solution.py:52
  87.7 2.9 copy-start.5
  90.5 271.5 %reduce-scatter.2.cloned.1.call-start = ((), (), s32[]{:S(2)}) async-start(), calls=%async_computation.4 | async-start | bytes 2949120 | tf_op jit(solution)/shard_map/reduce_scatter | solution.py:101
  181.0 1.7 copy-start.4
  192.7 8.1 %copy-start.7 = (bf16[6144,8]{0,1:T(8,128)(2,1)S(1)}, bf16[6144,8]{0,1:T(8,128)(2,1)}, u32[]{:S(2)}) copy-start(bf16[6144,8]{0,1:T(8,128)(2,1)} %param.18) | copy-start | bytes 294916
  212.0 22.7 %collective-permute-start.4 = (bf16[384,1024]{1,0:T(8,128)(2,1)S(1)}, bf16[384,1024]{1,0:T(8,128)(2,1)S(1)}, u32[]{:S(2)}, u32[]{:S(2)}) collective-permute-start(bf16[384,1024]{1,0:T(8,128)(2,1)S(1)} %fusion.44), channel_id=1, source_target_pairs={{0,1},{1,2},{2,3},{3,0},{4,5},{5,6},{6,7},{7,4},{8,9},{9,10},{10,1... | collective-permute-start | bytes 2359304 | tf_op jit(solution)/shard_map/ppermute | solution.py:19
  223.5 28.1 %collective-permute-start.1 = (bf16[384,1024]{1,0:T(8,128)(2,1)S(1)}, bf16[384,1024]{1,0:T(8,128)(2,1)}, u32[]{:S(2)}, u32[]{:S(2)}) collective-permute-start(bf16[384,1024]{1,0:T(8,128)(2,1)S(1)} %fusion.48), channel_id=1, source_target_pairs={{0,1},{1,2},{2,3},{3,0},{4,5},{5,6},{6,7},{7,4},{8,9},{9,10},{10,1... | collective-permute-start | bytes 2359304 | tf_op jit(solution)/shard_map/ppermute | solution.py:19
  224.1 44.4 %collective-permute-start.6 = (bf16[384,1024]{1,0:T(8,128)(2,1)S(1)}, bf16[384,1024]{1,0:T(8,128)(2,1)}, u32[]{:S(2)}, u32[]{:S(2)}) collective-permute-start(bf16[384,1024]{1,0:T(8,128)(2,1)S(1)} %fusion.44), channel_id=1, source_target_pairs={{0,3},{1,0},{2,1},{3,2},{4,7},{5,4},{6,5},{7,6},{8,11},{9,8},{10,9... | collective-permute-start | bytes 2359304 | tf_op jit(solution)/shard_map/ppermute | solution.py:21
  234.7 50.6 %collective-permute-start.5 = (bf16[384,1024]{1,0:T(8,128)(2,1)S(1)}, bf16[384,1024]{1,0:T(8,128)(2,1)}, u32[]{:S(2)}, u32[]{:S(2)}) collective-permute-start(bf16[384,1024]{1,0:T(8,128)(2,1)S(1)} %collective-permute-done.4), channel_id=1, source_target_pairs={{0,1},{1,2},{2,3},{3,0},{4,5},{5,6},{6,7},{7,4},{8,9},{9,10},{10,1... | collective-permute-start | bytes 2359304 | tf_op jit(solution)/shard_map/ppermute | solution.py:19
  234.7 67.2 %collective-permute-start.3 = (bf16[384,1024]{1,0:T(8,128)(2,1)S(1)}, bf16[384,1024]{1,0:T(8,128)(2,1)S(1)}, u32[]{:S(2)}, u32[]{:S(2)}) collective-permute-start(bf16[384,1024]{1,0:T(8,128)(2,1)S(1)} %fusion.48), channel_id=1, source_target_pairs={{0,3},{1,0},{2,1},{3,2},{4,7},{5,4},{6,5},{7,6},{8,11},{9,8},{10,9... | collective-permute-start | bytes 2359304 | tf_op jit(solution)/shard_map/ppermute | solution.py:21
  251.5 65.4 %collective-permute-start.2 = (bf16[384,1024]{1,0:T(8,128)(2,1)}, bf16[384,1024]{1,0:T(8,128)(2,1)S(1)}, u32[]{:S(2)}, u32[]{:S(2)}) collective-permute-start(bf16[384,1024]{1,0:T(8,128)(2,1)} %collective-permute-done.1), channel_id=1, source_target_pairs={{0,1},{1,2},{2,3},{3,0},{4,5},{5,6},{6,7},{7,4},{8,9},{9,10},{10,1... | collective-permute-start | bytes 2359304 | tf_op jit(solution)/shard_map/ppermute | solution.py:19
  316.9 47.0 %copy-start.1 = (bf16[8,2,64,1024]{3,2,1,0:T(8,128)(2,1)S(1)}, bf16[8,2,64,1024]{3,2,1,0:T(8,128)(2,1)}, u32[]{:S(2)}) copy-start(bf16[8,2,64,1024]{3,2,1,0:T(8,128)(2,1)} %param.23) | copy-start | bytes 6291460
Sparse Core Ops, SparseCore 0:
  8.9 22.3 all-gather.2
  34.7 50.4 all-gather.4
  90.7 88.7 all-reduce.1
  331.7 30.3 reduce-scatter.1
